TPU v7x, 512 devices: a whole 4x4x16 slice. The times are simulated.
512 devices in a mesh: sect: 8 (over x, y_hi), blk: 64 (over z, y_lo, core).
Axes of the slice: x: 4, y: 4 (y_hi: 2, y_lo: 2; y = y_hi * 2 + y_lo), z: 16, core: 2. Of those that a mesh axis runs over, the one named last changes fastest.
Arguments:
- bits: int32 [8, 1024], P('sect', 'blk'), may hold values from 0 to 1
- labels: int32 [128], replicated, may hold values from 0 to 127, each once
- left: bfloat16 [1024, 16384], P('blk')
- tensors: bfloat16 [8, 2, 128, 128, 128], P('sect', None, 'blk')
Outputs:
- prob: float32 [8, 1024], P('sect', 'blk')
- logprob: float32 [8, 1024], P('sect', 'blk')
Inputs may be any that keep to these rules, and one draw needn't show every extreme that they name: Every charge labels exactly one block.
All inputs are finite; a program needn't handle non-finite values.
Results may differ from a plain program's by a relative error of at most 0.0003.
Values may be sent and summed in bfloat16 or wider, within the bound.
No kernel may reach another device: no remote copies, remote signals or barrier semaphores. Data moves between devices by JAX's collectives and lax.ppermute only.
A program may use at most 64 MiB of HBM per device.

v0:
```python
import jax
import jax.numpy as jnp
from jax import lax
from jax.sharding import PartitionSpec as P


def passed_along(value, axis, steps):
    count = lax.axis_size(axis)
    first, last = (max(0, -steps), min(count, count - steps))
    return lax.ppermute(value, axis, [(source, source + steps) for source in range(first, last)])


def charge_order(labels, left, block):
    count_blocks = labels.shape[0]
    samples_here = left.shape[0]
    blocks = left.reshape(samples_here, count_blocks, block)
    index = jnp.arange(count_blocks, dtype=jnp.int32)
    pick = (labels[None, :] == index[:, None]).astype(jnp.bfloat16)
    ordered = jnp.einsum("ci,rik->rck", pick, blocks, preferred_element_type=jnp.float32)
    return ordered.astype(jnp.bfloat16)


def site_images(state, weights, block):
    count_rows = state.shape[0]
    blocks = state.reshape(count_rows, weights.shape[1], block)
    return jnp.einsum(
        "rck,bckl->brcl",
        blocks,
        weights,
        preferred_element_type=jnp.float32,
        precision=lax.Precision.HIGHEST,
    )


def run_sections(start_rows, site_bits, advance, count):
    segment = lax.axis_index("sect")
    segments = lax.axis_size("sect")
    mrows = start_rows.shape[1]

    def one_step(step, carry):
        state, total, prob_out, log_out = carry
        group = step - segment
        valid = (group >= 0) & (group < count)
        slot = jnp.clip(group, 0, count - 1)
        first = segment == 0
        start_now = lax.dynamic_index_in_dim(start_rows, slot, 0, keepdims=False)
        state = jnp.where(first, start_now, state)
        total = jnp.where(first, jnp.zeros_like(total), total)
        bit_rows = lax.dynamic_index_in_dim(site_bits, slot, 0, keepdims=False)
        prob, next_state = advance(state, bit_rows)
        total = total + jnp.log(prob)
        old_prob = lax.dynamic_index_in_dim(prob_out, slot, 0, keepdims=False)
        old_log = lax.dynamic_index_in_dim(log_out, slot, 0, keepdims=False)
        prob_out = lax.dynamic_update_index_in_dim(
            prob_out, jnp.where(valid, prob, old_prob), slot, 0
        )
        log_out = lax.dynamic_update_index_in_dim(
            log_out, jnp.where(valid, total, old_log), slot, 0
        )
        state, total = passed_along((next_state, total), "sect", 1)
        return (state, total, prob_out, log_out)

    empty = jnp.zeros((count, mrows), jnp.float32)
    init = (start_rows[0], jnp.zeros((mrows,), jnp.float32), empty, empty)
    result = lax.fori_loop(0, count + segments - 1, one_step, init)
    return (result[2], result[3])


def body(bits, labels, left, tensors):
    block = tensors.shape[-1]
    count_blocks = labels.shape[0]
    width = count_blocks * block
    rows = bits.shape[1]
    ordered = charge_order(labels, left, block)
    count = 1
    whole = lax.all_gather(tensors, "blk", axis=2, tiled=True)[0]

    def advance(state, bit_rows):
        image = site_images(state, whole, block)
        stay = image[0]
        raised = jnp.roll(image[1], 1, axis=1)
        norm_zero = jnp.sum(stay * stay, axis=(1, 2))
        norm_one = jnp.sum(raised * raised, axis=(1, 2))
        choose = bit_rows == 1
        chosen_norm = jnp.where(choose, norm_one, norm_zero)
        prob = chosen_norm / (norm_zero + norm_one)
        chosen = jnp.where(choose[:, None, None], raised, stay)
        scaled = chosen * lax.rsqrt(chosen_norm / width + 1e-06)[:, None, None]
        return (prob, scaled.reshape(state.shape[0], width))

    mrows = rows // count
    start_rows = ordered.astype(jnp.float32).reshape(count, mrows, width)
    site_bits = bits[0].reshape(count, mrows)
    prob_out, log_out = run_sections(start_rows, site_bits, advance, count)
    return (prob_out, log_out)


def solution(mesh):
    in_specs = (P("sect", "blk"), P(), P("blk", None), P("sect", None, "blk", None, None))
    out_specs = (P("sect", "blk"), P("sect", "blk"))
    return jax.shard_map(body, mesh=mesh, in_specs=in_specs, out_specs=out_specs, check_vma=False)
```

profile of v0, /device:TPU:2, one launch (start us, length us, event | category | flops | bytes accessed | tf_op | source)
XLA Modules:
  0.0 439.7 jit_solution(6856353192765204653)
XLA Ops:
  12.8 130.9 %all-gather.2.cloned.1.call-done = bf16[1,2,128,128,128]{4,3,1,0,2:T(8,128)(2,1)} async-done(((bf16[1,2,2,128,128]{4,3,1,0,2:T(8,128)(2,1)}), bf16[1,2,128,128,128]{4,3,1,0,2:T(8,128)(2,1)}) %all-gather.2.cloned.1.call-update) | async-done | bytes 8388624 | tf_op jit(solution)/shard_map/all_gather | solution.py:76
  143.7 288.7 %while.21 = (s32[]{:T(128)}, f32[16,16384]{1,0:T(8,128)S(1)}, f32[16]{0:T(128)S(1)}, f32[1,16]{1,0:T(1,128)S(1)}, f32[1,16]{1,0:T(1,128)S(1)}, /*index=5*/s32[1,...) while((s32[]{:T(128)}, f32[16,16384]{1,0:T(8,128)S(1)}, ...), condition=%wide.region_3.4_spmd.clone, body=%wide.region_0.3_spmd.clone.sunk | while | flops 807403776 | bytes 34604904 | solution.py:65
  145.2 6.5 %convolution_bitcast_fusion.2 = f32[2,16,128,128]{3,1,0,2:T(8,128)S(1)} fusion(bf16[2,128,128,128]{3,2,0,1:T(8,128)(2,1)} %get-tuple-element.370, f32[16,128,128,1]{2,1,0,3:T(8,128)S(1)} %bitcast.81), kind=kOutput, calls=%fused_computation.clone.1 | convolution fusion | flops 805306368 | bytes 11534336 | tf_op jit(solution)/shard_map/while/body/eval_jaxpr/rck,bckl->brcl/dot_general | solution.py:26
  161.7 21.4 %collective-permute-done.1 = f32[16]{0:T(128)S(1)} collective-permute-done((f32[16]{0:T(128)S(1)}, f32[16]{0:T(128)S(1)}, u32[]{:S(2)}, u32[]{:S(2)}) %collective-permute-start.1) | collective-permute-done | bytes 96 | tf_op jit(solution)/shard_map/while/body/eval_jaxpr/ppermute | solution.py:10
  184.7 6.5 %convolution_bitcast_fusion.2 = f32[2,16,128,128]{3,1,0,2:T(8,128)S(1)} fusion(bf16[2,128,128,128]{3,2,0,1:T(8,128)(2,1)} %get-tuple-element.370, f32[16,128,128,1]{2,1,0,3:T(8,128)S(1)} %bitcast.81), kind=kOutput, calls=%fused_computation.clone.1 | convolution fusion | flops 805306368 | bytes 11534336 | tf_op jit(solution)/shard_map/while/body/eval_jaxpr/rck,bckl->brcl/dot_general | solution.py:26
  201.2 20.5 %collective-permute-done.1 = f32[16]{0:T(128)S(1)} collective-permute-done((f32[16]{0:T(128)S(1)}, f32[16]{0:T(128)S(1)}, u32[]{:S(2)}, u32[]{:S(2)}) %collective-permute-start.1) | collective-permute-done | bytes 96 | tf_op jit(solution)/shard_map/while/body/eval_jaxpr/ppermute | solution.py:10
  223.2 6.5 %convolution_bitcast_fusion.2 = f32[2,16,128,128]{3,1,0,2:T(8,128)S(1)} fusion(bf16[2,128,128,128]{3,2,0,1:T(8,128)(2,1)} %get-tuple-element.370, f32[16,128,128,1]{2,1,0,3:T(8,128)S(1)} %bitcast.81), kind=kOutput, calls=%fused_computation.clone.1 | convolution fusion | flops 805306368 | bytes 11534336 | tf_op jit(solution)/shard_map/while/body/eval_jaxpr/rck,bckl->brcl/dot_general | solution.py:26
  234.3 5.4 %collective-permute-start.1 = (f32[16]{0:T(128)S(1)}, f32[16]{0:T(128)S(1)}, u32[]{:S(2)}, u32[]{:S(2)}) collective-permute-start(f32[16]{0:T(128)S(1)} %get-tuple-element.336), channel_id=1, source_target_pairs={{0,64},{64,128},{128,192},{192,256},{256,320},{320,384},{384,448},... | collective-permute-start | bytes 200 | tf_op jit(solution)/shard_map/while/body/eval_jaxpr/ppermute | solution.py:10
  239.8 19.5 %collective-permute-done.1 = f32[16]{0:T(128)S(1)} collective-permute-done((f32[16]{0:T(128)S(1)}, f32[16]{0:T(128)S(1)}, u32[]{:S(2)}, u32[]{:S(2)}) %collective-permute-start.1) | collective-permute-done | bytes 96 | tf_op jit(solution)/shard_map/while/body/eval_jaxpr/ppermute | solution.py:10
  260.8 6.5 %convolution_bitcast_fusion.2 = f32[2,16,128,128]{3,1,0,2:T(8,128)S(1)} fusion(bf16[2,128,128,128]{3,2,0,1:T(8,128)(2,1)} %get-tuple-element.370, f32[16,128,128,1]{2,1,0,3:T(8,128)S(1)} %bitcast.81), kind=kOutput, calls=%fused_computation.clone.1 | convolution fusion | flops 805306368 | bytes 11534336 | tf_op jit(solution)/shard_map/while/body/eval_jaxpr/rck,bckl->brcl/dot_general | solution.py:26
  271.0 6.3 %collective-permute-start.1 = (f32[16]{0:T(128)S(1)}, f32[16]{0:T(128)S(1)}, u32[]{:S(2)}, u32[]{:S(2)}) collective-permute-start(f32[16]{0:T(128)S(1)} %get-tuple-element.336), channel_id=1, source_target_pairs={{0,64},{64,128},{128,192},{192,256},{256,320},{320,384},{384,448},... | collective-permute-start | bytes 200 | tf_op jit(solution)/shard_map/while/body/eval_jaxpr/ppermute | solution.py:10
  277.3 18.5 %collective-permute-done.1 = f32[16]{0:T(128)S(1)} collective-permute-done((f32[16]{0:T(128)S(1)}, f32[16]{0:T(128)S(1)}, u32[]{:S(2)}, u32[]{:S(2)}) %collective-permute-start.1) | collective-permute-done | bytes 96 | tf_op jit(solution)/shard_map/while/body/eval_jaxpr/ppermute | solution.py:10
  297.4 6.5 %convolution_bitcast_fusion.2 = f32[2,16,128,128]{3,1,0,2:T(8,128)S(1)} fusion(bf16[2,128,128,128]{3,2,0,1:T(8,128)(2,1)} %get-tuple-element.370, f32[16,128,128,1]{2,1,0,3:T(8,128)S(1)} %bitcast.81), kind=kOutput, calls=%fused_computation.clone.1 | convolution fusion | flops 805306368 | bytes 11534336 | tf_op jit(solution)/shard_map/while/body/eval_jaxpr/rck,bckl->brcl/dot_general | solution.py:26
  307.6 6.3 %collective-permute-start.1 = (f32[16]{0:T(128)S(1)}, f32[16]{0:T(128)S(1)}, u32[]{:S(2)}, u32[]{:S(2)}) collective-permute-start(f32[16]{0:T(128)S(1)} %get-tuple-element.336), channel_id=1, source_target_pairs={{0,64},{64,128},{128,192},{192,256},{256,320},{320,384},{384,448},... | collective-permute-start | bytes 200 | tf_op jit(solution)/shard_map/while/body/eval_jaxpr/ppermute | solution.py:10
  313.9 17.5 %collective-permute-done.1 = f32[16]{0:T(128)S(1)} collective-permute-done((f32[16]{0:T(128)S(1)}, f32[16]{0:T(128)S(1)}, u32[]{:S(2)}, u32[]{:S(2)}) %collective-permute-start.1) | collective-permute-done | bytes 96 | tf_op jit(solution)/shard_map/while/body/eval_jaxpr/ppermute | solution.py:10
  333.0 6.5 %convolution_bitcast_fusion.2 = f32[2,16,128,128]{3,1,0,2:T(8,128)S(1)} fusion(bf16[2,128,128,128]{3,2,0,1:T(8,128)(2,1)} %get-tuple-element.370, f32[16,128,128,1]{2,1,0,3:T(8,128)S(1)} %bitcast.81), kind=kOutput, calls=%fused_computation.clone.1 | convolution fusion | flops 805306368 | bytes 11534336 | tf_op jit(solution)/shard_map/while/body/eval_jaxpr/rck,bckl->brcl/dot_general | solution.py:26
  343.2 6.3 %collective-permute-start.1 = (f32[16]{0:T(128)S(1)}, f32[16]{0:T(128)S(1)}, u32[]{:S(2)}, u32[]{:S(2)}) collective-permute-start(f32[16]{0:T(128)S(1)} %get-tuple-element.336), channel_id=1, source_target_pairs={{0,64},{64,128},{128,192},{192,256},{256,320},{320,384},{384,448},... | collective-permute-start | bytes 200 | tf_op jit(solution)/shard_map/while/body/eval_jaxpr/ppermute | solution.py:10
  349.6 16.5 %collective-permute-done.1 = f32[16]{0:T(128)S(1)} collective-permute-done((f32[16]{0:T(128)S(1)}, f32[16]{0:T(128)S(1)}, u32[]{:S(2)}, u32[]{:S(2)}) %collective-permute-start.1) | collective-permute-done | bytes 96 | tf_op jit(solution)/shard_map/while/body/eval_jaxpr/ppermute | solution.py:10
  367.6 6.5 %convolution_bitcast_fusion.2 = f32[2,16,128,128]{3,1,0,2:T(8,128)S(1)} fusion(bf16[2,128,128,128]{3,2,0,1:T(8,128)(2,1)} %get-tuple-element.370, f32[16,128,128,1]{2,1,0,3:T(8,128)S(1)} %bitcast.81), kind=kOutput, calls=%fused_computation.clone.1 | convolution fusion | flops 805306368 | bytes 11534336 | tf_op jit(solution)/shard_map/while/body/eval_jaxpr/rck,bckl->brcl/dot_general | solution.py:26
  377.8 6.3 %collective-permute-start.1 = (f32[16]{0:T(128)S(1)}, f32[16]{0:T(128)S(1)}, u32[]{:S(2)}, u32[]{:S(2)}) collective-permute-start(f32[16]{0:T(128)S(1)} %get-tuple-element.336), channel_id=1, source_target_pairs={{0,64},{64,128},{128,192},{192,256},{256,320},{320,384},{384,448},... | collective-permute-start | bytes 200 | tf_op jit(solution)/shard_map/while/body/eval_jaxpr/ppermute | solution.py:10
  384.2 15.5 %collective-permute-done.1 = f32[16]{0:T(128)S(1)} collective-permute-done((f32[16]{0:T(128)S(1)}, f32[16]{0:T(128)S(1)}, u32[]{:S(2)}, u32[]{:S(2)}) %collective-permute-start.1) | collective-permute-done | bytes 96 | tf_op jit(solution)/shard_map/while/body/eval_jaxpr/ppermute | solution.py:10
  401.3 6.5 %convolution_bitcast_fusion.2 = f32[2,16,128,128]{3,1,0,2:T(8,128)S(1)} fusion(bf16[2,128,128,128]{3,2,0,1:T(8,128)(2,1)} %get-tuple-element.370, f32[16,128,128,1]{2,1,0,3:T(8,128)S(1)} %bitcast.81), kind=kOutput, calls=%fused_computation.clone.1 | convolution fusion | flops 805306368 | bytes 11534336 | tf_op jit(solution)/shard_map/while/body/eval_jaxpr/rck,bckl->brcl/dot_general | solution.py:26
  411.4 6.3 %collective-permute-start.1 = (f32[16]{0:T(128)S(1)}, f32[16]{0:T(128)S(1)}, u32[]{:S(2)}, u32[]{:S(2)}) collective-permute-start(f32[16]{0:T(128)S(1)} %get-tuple-element.336), channel_id=1, source_target_pairs={{0,64},{64,128},{128,192},{192,256},{256,320},{320,384},{384,448},... | collective-permute-start | bytes 200 | tf_op jit(solution)/shard_map/while/body/eval_jaxpr/ppermute | solution.py:10
  417.8 14.6 %collective-permute-done.1 = f32[16]{0:T(128)S(1)} collective-permute-done((f32[16]{0:T(128)S(1)}, f32[16]{0:T(128)S(1)}, u32[]{:S(2)}, u32[]{:S(2)}) %collective-permute-start.1) | collective-permute-done | bytes 96 | tf_op jit(solution)/shard_map/while/body/eval_jaxpr/ppermute | solution.py:10
  (136 shorter events, 61.2 us)
Async XLA Ops:
  7.2 136.5 %all-gather.2.cloned.1.call-start = ((), (), s32[]{:S(2)}) async-start(), calls=%async_computation | async-start | bytes 8519680 | tf_op jit(solution)/shard_map/all_gather | solution.py:76
  151.7 0.8 copy-start
  153.4 29.7 %collective-permute-start = (f32[16,16384]{1,0:T(8,128)S(1)}, f32[16,16384]{1,0:T(8,128)S(1)}, u32[]{:S(2)}, u32[]{:S(2)}) collective-permute-start(f32[16,16384]{1,0:T(8,128)S(1)} %fusion.23), channel_id=1, source_target_pairs={{0,64},{64,128},{128,192},{192,256},{256,320},{320,384},{384,448},... | collective-permute-start | bytes 3145736 | tf_op jit(solution)/shard_map/while/body/eval_jaxpr/ppermute | solution.py:10
  158.1 25.0 %collective-permute-start.1 = (f32[16]{0:T(128)S(1)}, f32[16]{0:T(128)S(1)}, u32[]{:S(2)}, u32[]{:S(2)}) collective-permute-start(f32[16]{0:T(128)S(1)} %get-tuple-element.336), channel_id=1, source_target_pairs={{0,64},{64,128},{128,192},{192,256},{256,320},{320,384},{384,448},... | collective-permute-start | bytes 200 | tf_op jit(solution)/shard_map/while/body/eval_jaxpr/ppermute | solution.py:10
  191.1 0.8 copy-start
  192.9 28.8 %collective-permute-start = (f32[16,16384]{1,0:T(8,128)S(1)}, f32[16,16384]{1,0:T(8,128)S(1)}, u32[]{:S(2)}, u32[]{:S(2)}) collective-permute-start(f32[16,16384]{1,0:T(8,128)S(1)} %fusion.23), channel_id=1, source_target_pairs={{0,64},{64,128},{128,192},{192,256},{256,320},{320,384},{384,448},... | collective-permute-start | bytes 3145736 | tf_op jit(solution)/shard_map/while/body/eval_jaxpr/ppermute | solution.py:10
  196.7 25.0 %collective-permute-start.1 = (f32[16]{0:T(128)S(1)}, f32[16]{0:T(128)S(1)}, u32[]{:S(2)}, u32[]{:S(2)}) collective-permute-start(f32[16]{0:T(128)S(1)} %get-tuple-element.336), channel_id=1, source_target_pairs={{0,64},{64,128},{128,192},{192,256},{256,320},{320,384},{384,448},... | collective-permute-start | bytes 200 | tf_op jit(solution)/shard_map/while/body/eval_jaxpr/ppermute | solution.py:10
  229.7 0.8 copy-start
  231.5 27.8 %collective-permute-start = (f32[16,16384]{1,0:T(8,128)S(1)}, f32[16,16384]{1,0:T(8,128)S(1)}, u32[]{:S(2)}, u32[]{:S(2)}) collective-permute-start(f32[16,16384]{1,0:T(8,128)S(1)} %fusion.23), channel_id=1, source_target_pairs={{0,64},{64,128},{128,192},{192,256},{256,320},{320,384},{384,448},... | collective-permute-start | bytes 3145736 | tf_op jit(solution)/shard_map/while/body/eval_jaxpr/ppermute | solution.py:10
  234.3 24.9 %collective-permute-start.1 = (f32[16]{0:T(128)S(1)}, f32[16]{0:T(128)S(1)}, u32[]{:S(2)}, u32[]{:S(2)}) collective-permute-start(f32[16]{0:T(128)S(1)} %get-tuple-element.336), channel_id=1, source_target_pairs={{0,64},{64,128},{128,192},{192,256},{256,320},{320,384},{384,448},... | collective-permute-start | bytes 200 | tf_op jit(solution)/shard_map/while/body/eval_jaxpr/ppermute | solution.py:10
  267.3 0.8 copy-start
  269.1 26.8 %collective-permute-start = (f32[16,16384]{1,0:T(8,128)S(1)}, f32[16,16384]{1,0:T(8,128)S(1)}, u32[]{:S(2)}, u32[]{:S(2)}) collective-permute-start(f32[16,16384]{1,0:T(8,128)S(1)} %fusion.23), channel_id=1, source_target_pairs={{0,64},{64,128},{128,192},{192,256},{256,320},{320,384},{384,448},... | collective-permute-start | bytes 3145736 | tf_op jit(solution)/shard_map/while/body/eval_jaxpr/ppermute | solution.py:10
  271.0 24.8 %collective-permute-start.1 = (f32[16]{0:T(128)S(1)}, f32[16]{0:T(128)S(1)}, u32[]{:S(2)}, u32[]{:S(2)}) collective-permute-start(f32[16]{0:T(128)S(1)} %get-tuple-element.336), channel_id=1, source_target_pairs={{0,64},{64,128},{128,192},{192,256},{256,320},{320,384},{384,448},... | collective-permute-start | bytes 200 | tf_op jit(solution)/shard_map/while/body/eval_jaxpr/ppermute | solution.py:10
  303.9 0.8 copy-start
  305.7 25.8 %collective-permute-start = (f32[16,16384]{1,0:T(8,128)S(1)}, f32[16,16384]{1,0:T(8,128)S(1)}, u32[]{:S(2)}, u32[]{:S(2)}) collective-permute-start(f32[16,16384]{1,0:T(8,128)S(1)} %fusion.23), channel_id=1, source_target_pairs={{0,64},{64,128},{128,192},{192,256},{256,320},{320,384},{384,448},... | collective-permute-start | bytes 3145736 | tf_op jit(solution)/shard_map/while/body/eval_jaxpr/ppermute | solution.py:10
  307.6 23.9 %collective-permute-start.1 = (f32[16]{0:T(128)S(1)}, f32[16]{0:T(128)S(1)}, u32[]{:S(2)}, u32[]{:S(2)}) collective-permute-start(f32[16]{0:T(128)S(1)} %get-tuple-element.336), channel_id=1, source_target_pairs={{0,64},{64,128},{128,192},{192,256},{256,320},{320,384},{384,448},... | collective-permute-start | bytes 200 | tf_op jit(solution)/shard_map/while/body/eval_jaxpr/ppermute | solution.py:10
  339.5 0.8 copy-start
  341.3 24.8 %collective-permute-start = (f32[16,16384]{1,0:T(8,128)S(1)}, f32[16,16384]{1,0:T(8,128)S(1)}, u32[]{:S(2)}, u32[]{:S(2)}) collective-permute-start(f32[16,16384]{1,0:T(8,128)S(1)} %fusion.23), channel_id=1, source_target_pairs={{0,64},{64,128},{128,192},{192,256},{256,320},{320,384},{384,448},... | collective-permute-start | bytes 3145736 | tf_op jit(solution)/shard_map/while/body/eval_jaxpr/ppermute | solution.py:10
  343.2 22.9 %collective-permute-start.1 = (f32[16]{0:T(128)S(1)}, f32[16]{0:T(128)S(1)}, u32[]{:S(2)}, u32[]{:S(2)}) collective-permute-start(f32[16]{0:T(128)S(1)} %get-tuple-element.336), channel_id=1, source_target_pairs={{0,64},{64,128},{128,192},{192,256},{256,320},{320,384},{384,448},... | collective-permute-start | bytes 200 | tf_op jit(solution)/shard_map/while/body/eval_jaxpr/ppermute | solution.py:10
  375.9 23.8 %collective-permute-start = (f32[16,16384]{1,0:T(8,128)S(1)}, f32[16,16384]{1,0:T(8,128)S(1)}, u32[]{:S(2)}, u32[]{:S(2)}) collective-permute-start(f32[16,16384]{1,0:T(8,128)S(1)} %fusion.23), channel_id=1, source_target_pairs={{0,64},{64,128},{128,192},{192,256},{256,320},{320,384},{384,448},... | collective-permute-start | bytes 3145736 | tf_op jit(solution)/shard_map/while/body/eval_jaxpr/ppermute | solution.py:10
  377.8 21.9 %collective-permute-start.1 = (f32[16]{0:T(128)S(1)}, f32[16]{0:T(128)S(1)}, u32[]{:S(2)}, u32[]{:S(2)}) collective-permute-start(f32[16]{0:T(128)S(1)} %get-tuple-element.336), channel_id=1, source_target_pairs={{0,64},{64,128},{128,192},{192,256},{256,320},{320,384},{384,448},... | collective-permute-start | bytes 200 | tf_op jit(solution)/shard_map/while/body/eval_jaxpr/ppermute | solution.py:10
  407.7 0.8 copy-start
  409.5 22.8 %collective-permute-start = (f32[16,16384]{1,0:T(8,128)S(1)}, f32[16,16384]{1,0:T(8,128)S(1)}, u32[]{:S(2)}, u32[]{:S(2)}) collective-permute-start(f32[16,16384]{1,0:T(8,128)S(1)} %fusion.23), channel_id=1, source_target_pairs={{0,64},{64,128},{128,192},{192,256},{256,320},{320,384},{384,448},... | collective-permute-start | bytes 3145736 | tf_op jit(solution)/shard_map/while/body/eval_jaxpr/ppermute | solution.py:10
  411.4 20.9 %collective-permute-start.1 = (f32[16]{0:T(128)S(1)}, f32[16]{0:T(128)S(1)}, u32[]{:S(2)}, u32[]{:S(2)}) collective-permute-start(f32[16]{0:T(128)S(1)} %get-tuple-element.336), channel_id=1, source_target_pairs={{0,64},{64,128},{128,192},{192,256},{256,320},{320,384},{384,448},... | collective-permute-start | bytes 200 | tf_op jit(solution)/shard_map/while/body/eval_jaxpr/ppermute | solution.py:10
  (3 other events, 1.8 us)
Sparse Core Ops, SparseCore 0:
  10.1 133.4 all-gather.1
where the time goes:
time: 441 us; the launch traced here: 440 us
  waiting for transfers between devices  275 us (62%)
  starting transfers between devices  66 us (15%)
  matrix products  52.6 us (12%)
  other arithmetic  21.2 us (5%)
  between operations  14.1 us (3%)
  local copies, waits for them, and re-layouts  10 us (2%)
    ppermute x16, waiting for transfers between devices, passed_along(): lax.ppermute(value, axis, [(source, source + steps) for source in range(f...  144 us
    all_gather x1, waiting for transfers between devices, body(): whole = lax.all_gather(tensors, 'blk', axis=2, tiled=True)[0]  131 us
    ppermute x16, starting transfers between devices, passed_along(): lax.ppermute(value, axis, [(source, source + steps) for source in range(f...  66 us
    dot_general x8, matrix products, site_images(): jnp.einsum('rck,bckl->brcl', blocks, weights, preferred_element_type=jnp....  51.7 us
    while x8, other arithmetic  10.6 us
  transfers between devices with their start and end apart: 17, of which 9 were waited for; matrix products, arithmetic and copies ran while one was open for 1% of the time, Pallas kernels for 0%

commit v1 on v0

--- a/solution.py
+++ b/solution.py
@@ -73,7 +73,9 @@
     rows = bits.shape[1]
     ordered = charge_order(labels, left, block)
     count = 1
-    whole = lax.all_gather(tensors, "blk", axis=2, tiled=True)[0]
+    whole = jnp.concatenate(
+        lax.all_to_all(jnp.stack([tensors] * lax.axis_size("blk")), "blk", 0, 0), axis=2
+    )[0]
 
     def advance(state, bit_rows):
         image = site_images(state, whole, block)

time: 441 us -> 691 us (1.57)
  the two profiles are of different devices: /device:TPU:2 before, /device:TPU:46 now
where the time goes in v1:
time: 691 us; the launch traced here: 690 us
  waiting for transfers between devices  542 us (78%)
  matrix products  51.9 us (8%)
  starting transfers between devices  51.8 us (7%)
  other arithmetic  29.9 us (4%)
  local copies, waits for them, and re-layouts  13.6 us (2%)
    all_to_all x1, waiting for transfers between devices, body(): lax.all_to_all(jnp.stack([tensors] * lax.axis_size('blk')), 'blk', 0, 0)  367 us
    ppermute x16, waiting for transfers between devices, passed_along(): lax.ppermute(value, axis, [(source, source + steps) for source in range(f...  174 us
    dot_general x8, matrix products, site_images(): jnp.einsum('rck,bckl->brcl', blocks, weights, preferred_element_type=jnp....  51.6 us
    ppermute x16, starting transfers between devices, passed_along(): lax.ppermute(value, axis, [(source, source + steps) for source in range(f...  34.8 us
    all_to_all x1, starting transfers between devices, body(): lax.all_to_all(jnp.stack([tensors] * lax.axis_size('blk')), 'blk', 0, 0)  17 us
  transfers between devices with their start and end apart: 17, of which 9 were waited for; matrix products, arithmetic and copies ran while one was open for 0% of the time, Pallas kernels for 0%

profile of v1, /device:TPU:46, one launch (start us, length us, event | category | flops | bytes accessed | tf_op | source)
XLA Modules:
  0.0 690.0 jit_solution(10885809408844647569)
XLA Ops:
  1.5 5.3 stack.2
  6.9 17.0 %all-to-all-start = ((bf16[64,1,2,2,128,128]{5,4,2,3,1,0:T(8,128)(2,1)}), bf16[64,1,2,2,128,128]{5,4,2,3,1,0:T(8,128)(2,1)}, u32[]{:S(2)}, u32[]{:S(2)}) async-start(bf16[64,1,2,2,128,128]{5,4,2,3,1,0:T(8,128)(2,1)} %stack.2), calls=%async_computation | async-start | bytes 16777216 | tf_op jit(solution)/shard_map/all_to_all | solution.py:77
  26.1 367.3 %all-to-all-done = bf16[64,1,2,2,128,128]{5,4,2,3,1,0:T(8,128)(2,1)} async-done(((bf16[64,1,2,2,128,128]{5,4,2,3,1,0:T(8,128)(2,1)}), bf16[64,1,2,2,128,128]{5,4,2,3,1,0:T(8,128)(2,1)}, u32[]{:S(2)}, u32[]{:S(2)}) %all-to-all-start) | async-done | bytes 8388640 | tf_op jit(solution)/shard_map/all_to_all | solution.py:77
  393.3 296.1 %while.21 = (s32[]{:T(128)}, f32[16,16384]{1,0:T(8,128)S(1)}, f32[16]{0:T(128)S(1)}, f32[1,16]{1,0:T(1,128)S(1)}, f32[1,16]{1,0:T(1,128)S(1)}, /*index=5*/s32[1,...) while((s32[]{:T(128)}, f32[16,16384]{1,0:T(8,128)S(1)}, ...), condition=%wide.region_3.4_spmd.clone, body=%wide.region_0.3_spmd.clone.sunk | while | flops 807403776 | bytes 34604624 | solution.py:65
  394.9 6.4 convolution_bitcast_fusion.2
  404.2 4.2 collective-permute-start
  410.3 23.4 %collective-permute-done.1 = f32[16]{0:T(128)S(1)} collective-permute-done((f32[16]{0:T(128)S(1)}, f32[16]{0:T(128)S(1)}, u32[]{:S(2)}, u32[]{:S(2)}) %collective-permute-start.1) | collective-permute-done | bytes 96 | tf_op jit(solution)/shard_map/while/body/eval_jaxpr/ppermute | solution.py:10
  435.3 6.4 convolution_bitcast_fusion.2
  444.6 3.3 collective-permute-start
  447.9 1.9 collective-permute-start.1
  449.9 23.4 %collective-permute-done.1 = f32[16]{0:T(128)S(1)} collective-permute-done((f32[16]{0:T(128)S(1)}, f32[16]{0:T(128)S(1)}, u32[]{:S(2)}, u32[]{:S(2)}) %collective-permute-start.1) | collective-permute-done | bytes 96 | tf_op jit(solution)/shard_map/while/body/eval_jaxpr/ppermute | solution.py:10
  474.8 6.4 convolution_bitcast_fusion.2
  484.1 2.4 collective-permute-start
  488.4 23.3 %collective-permute-done.1 = f32[16]{0:T(128)S(1)} collective-permute-done((f32[16]{0:T(128)S(1)}, f32[16]{0:T(128)S(1)}, u32[]{:S(2)}, u32[]{:S(2)}) %collective-permute-start.1) | collective-permute-done | bytes 96 | tf_op jit(solution)/shard_map/while/body/eval_jaxpr/ppermute | solution.py:10
  513.3 6.4 convolution_bitcast_fusion.2
  526.5 22.8 %collective-permute-done.1 = f32[16]{0:T(128)S(1)} collective-permute-done((f32[16]{0:T(128)S(1)}, f32[16]{0:T(128)S(1)}, u32[]{:S(2)}, u32[]{:S(2)}) %collective-permute-start.1) | collective-permute-done | bytes 96 | tf_op jit(solution)/shard_map/while/body/eval_jaxpr/ppermute | solution.py:10
  550.8 6.4 convolution_bitcast_fusion.2
  564.0 21.8 %collective-permute-done.1 = f32[16]{0:T(128)S(1)} collective-permute-done((f32[16]{0:T(128)S(1)}, f32[16]{0:T(128)S(1)}, u32[]{:S(2)}, u32[]{:S(2)}) %collective-permute-start.1) | collective-permute-done | bytes 96 | tf_op jit(solution)/shard_map/while/body/eval_jaxpr/ppermute | solution.py:10
  587.3 6.4 convolution_bitcast_fusion.2
  600.5 20.8 %collective-permute-done.1 = f32[16]{0:T(128)S(1)} collective-permute-done((f32[16]{0:T(128)S(1)}, f32[16]{0:T(128)S(1)}, u32[]{:S(2)}, u32[]{:S(2)}) %collective-permute-start.1) | collective-permute-done | bytes 96 | tf_op jit(solution)/shard_map/while/body/eval_jaxpr/ppermute | solution.py:10
  622.9 6.4 convolution_bitcast_fusion.2
  636.0 19.8 %collective-permute-done.1 = f32[16]{0:T(128)S(1)} collective-permute-done((f32[16]{0:T(128)S(1)}, f32[16]{0:T(128)S(1)}, u32[]{:S(2)}, u32[]{:S(2)}) %collective-permute-start.1) | collective-permute-done | bytes 96 | tf_op jit(solution)/shard_map/while/body/eval_jaxpr/ppermute | solution.py:10
  657.4 6.4 convolution_bitcast_fusion.2
  670.6 18.8 %collective-permute-done.1 = f32[16]{0:T(128)S(1)} collective-permute-done((f32[16]{0:T(128)S(1)}, f32[16]{0:T(128)S(1)}, u32[]{:S(2)}, u32[]{:S(2)}) %collective-permute-start.1) | collective-permute-done | bytes 96 | tf_op jit(solution)/shard_map/while/body/eval_jaxpr/ppermute | solution.py:10
  (126 shorter events, 61.4 us)
Async XLA Ops:
  6.9 17.0 %copy-start = (bf16[16,16384]{1,0:T(8,128)(2,1)S(1)}, bf16[16,16384]{1,0:T(8,128)(2,1)}, u32[]{:S(2)}) copy-start(bf16[16,16384]{1,0:T(8,128)(2,1)} %param.8) | copy-start | bytes 1572868
  6.9 17.1 %copy-start.4 = (s32[128]{0:T(128)S(1)}, s32[128]{0:T(128)}, u32[]{:S(2)}) copy-start(s32[128]{0:T(128)} %param.7) | copy-start | bytes 1540
  6.9 386.4 %copy-start.1 = (s32[1,16]{1,0:T(1,128)S(1)}, s32[1,16]{1,0:T(1,128)}, u32[]{:S(2)}) copy-start(s32[1,16]{1,0:T(1,128)} %param.6) | copy-start | bytes 196
  6.9 386.4 %all-to-all-start = ((bf16[64,1,2,2,128,128]{5,4,2,3,1,0:T(8,128)(2,1)}), bf16[64,1,2,2,128,128]{5,4,2,3,1,0:T(8,128)(2,1)}, u32[]{:S(2)}, u32[]{:S(2)}) async-start(bf16[64,1,2,2,128,128]{5,4,2,3,1,0:T(8,128)(2,1)} %stack.2), calls=%async_computation | async-start | bytes 16777216 | tf_op jit(solution)/shard_map/all_to_all | solution.py:77
  404.2 29.6 %collective-permute-start = (f32[16,16384]{1,0:T(8,128)}, f32[16,16384]{1,0:T(8,128)S(1)}, u32[]{:S(2)}, u32[]{:S(2)}) collective-permute-start(f32[16,16384]{1,0:T(8,128)} %fusion.23), channel_id=1, source_target_pairs={{0,64},{64,128},{128,192},{192,256},{256,320},{320,384},{384,448},... | collective-permute-start | bytes 3145736 | tf_op jit(solution)/shard_map/while/body/eval_jaxpr/ppermute | solution.py:10
  408.4 25.4 %collective-permute-start.1 = (f32[16]{0:T(128)S(1)}, f32[16]{0:T(128)S(1)}, u32[]{:S(2)}, u32[]{:S(2)}) collective-permute-start(f32[16]{0:T(128)S(1)} %get-tuple-element.336), channel_id=1, source_target_pairs={{0,64},{64,128},{128,192},{192,256},{256,320},{320,384},{384,448},... | collective-permute-start | bytes 200 | tf_op jit(solution)/shard_map/while/body/eval_jaxpr/ppermute | solution.py:10
  444.6 28.7 %collective-permute-start = (f32[16,16384]{1,0:T(8,128)}, f32[16,16384]{1,0:T(8,128)S(1)}, u32[]{:S(2)}, u32[]{:S(2)}) collective-permute-start(f32[16,16384]{1,0:T(8,128)} %fusion.23), channel_id=1, source_target_pairs={{0,64},{64,128},{128,192},{192,256},{256,320},{320,384},{384,448},... | collective-permute-start | bytes 3145736 | tf_op jit(solution)/shard_map/while/body/eval_jaxpr/ppermute | solution.py:10
  447.9 25.3 %collective-permute-start.1 = (f32[16]{0:T(128)S(1)}, f32[16]{0:T(128)S(1)}, u32[]{:S(2)}, u32[]{:S(2)}) collective-permute-start(f32[16]{0:T(128)S(1)} %get-tuple-element.336), channel_id=1, source_target_pairs={{0,64},{64,128},{128,192},{192,256},{256,320},{320,384},{384,448},... | collective-permute-start | bytes 200 | tf_op jit(solution)/shard_map/while/body/eval_jaxpr/ppermute | solution.py:10
  484.1 27.7 %collective-permute-start = (f32[16,16384]{1,0:T(8,128)}, f32[16,16384]{1,0:T(8,128)S(1)}, u32[]{:S(2)}, u32[]{:S(2)}) collective-permute-start(f32[16,16384]{1,0:T(8,128)} %fusion.23), channel_id=1, source_target_pairs={{0,64},{64,128},{128,192},{192,256},{256,320},{320,384},{384,448},... | collective-permute-start | bytes 3145736 | tf_op jit(solution)/shard_map/while/body/eval_jaxpr/ppermute | solution.py:10
  486.5 25.3 %collective-permute-start.1 = (f32[16]{0:T(128)S(1)}, f32[16]{0:T(128)S(1)}, u32[]{:S(2)}, u32[]{:S(2)}) collective-permute-start(f32[16]{0:T(128)S(1)} %get-tuple-element.336), channel_id=1, source_target_pairs={{0,64},{64,128},{128,192},{192,256},{256,320},{320,384},{384,448},... | collective-permute-start | bytes 200 | tf_op jit(solution)/shard_map/while/body/eval_jaxpr/ppermute | solution.py:10
  522.6 26.7 %collective-permute-start = (f32[16,16384]{1,0:T(8,128)}, f32[16,16384]{1,0:T(8,128)S(1)}, u32[]{:S(2)}, u32[]{:S(2)}) collective-permute-start(f32[16,16384]{1,0:T(8,128)} %fusion.23), channel_id=1, source_target_pairs={{0,64},{64,128},{128,192},{192,256},{256,320},{320,384},{384,448},... | collective-permute-start | bytes 3145736 | tf_op jit(solution)/shard_map/while/body/eval_jaxpr/ppermute | solution.py:10
  524.5 24.8 %collective-permute-start.1 = (f32[16]{0:T(128)S(1)}, f32[16]{0:T(128)S(1)}, u32[]{:S(2)}, u32[]{:S(2)}) collective-permute-start(f32[16]{0:T(128)S(1)} %get-tuple-element.336), channel_id=1, source_target_pairs={{0,64},{64,128},{128,192},{192,256},{256,320},{320,384},{384,448},... | collective-permute-start | bytes 200 | tf_op jit(solution)/shard_map/while/body/eval_jaxpr/ppermute | solution.py:10
  560.1 25.7 %collective-permute-start = (f32[16,16384]{1,0:T(8,128)}, f32[16,16384]{1,0:T(8,128)S(1)}, u32[]{:S(2)}, u32[]{:S(2)}) collective-permute-start(f32[16,16384]{1,0:T(8,128)} %fusion.23), channel_id=1, source_target_pairs={{0,64},{64,128},{128,192},{192,256},{256,320},{320,384},{384,448},... | collective-permute-start | bytes 3145736 | tf_op jit(solution)/shard_map/while/body/eval_jaxpr/ppermute | solution.py:10
  562.0 23.8 %collective-permute-start.1 = (f32[16]{0:T(128)S(1)}, f32[16]{0:T(128)S(1)}, u32[]{:S(2)}, u32[]{:S(2)}) collective-permute-start(f32[16]{0:T(128)S(1)} %get-tuple-element.336), channel_id=1, source_target_pairs={{0,64},{64,128},{128,192},{192,256},{256,320},{320,384},{384,448},... | collective-permute-start | bytes 200 | tf_op jit(solution)/shard_map/while/body/eval_jaxpr/ppermute | solution.py:10
  596.6 24.7 %collective-permute-start = (f32[16,16384]{1,0:T(8,128)}, f32[16,16384]{1,0:T(8,128)S(1)}, u32[]{:S(2)}, u32[]{:S(2)}) collective-permute-start(f32[16,16384]{1,0:T(8,128)} %fusion.23), channel_id=1, source_target_pairs={{0,64},{64,128},{128,192},{192,256},{256,320},{320,384},{384,448},... | collective-permute-start | bytes 3145736 | tf_op jit(solution)/shard_map/while/body/eval_jaxpr/ppermute | solution.py:10
  598.6 22.8 %collective-permute-start.1 = (f32[16]{0:T(128)S(1)}, f32[16]{0:T(128)S(1)}, u32[]{:S(2)}, u32[]{:S(2)}) collective-permute-start(f32[16]{0:T(128)S(1)} %get-tuple-element.336), channel_id=1, source_target_pairs={{0,64},{64,128},{128,192},{192,256},{256,320},{320,384},{384,448},... | collective-permute-start | bytes 200 | tf_op jit(solution)/shard_map/while/body/eval_jaxpr/ppermute | solution.py:10
  632.2 23.7 %collective-permute-start = (f32[16,16384]{1,0:T(8,128)}, f32[16,16384]{1,0:T(8,128)S(1)}, u32[]{:S(2)}, u32[]{:S(2)}) collective-permute-start(f32[16,16384]{1,0:T(8,128)} %fusion.23), channel_id=1, source_target_pairs={{0,64},{64,128},{128,192},{192,256},{256,320},{320,384},{384,448},... | collective-permute-start | bytes 3145736 | tf_op jit(solution)/shard_map/while/body/eval_jaxpr/ppermute | solution.py:10
  634.1 21.8 %collective-permute-start.1 = (f32[16]{0:T(128)S(1)}, f32[16]{0:T(128)S(1)}, u32[]{:S(2)}, u32[]{:S(2)}) collective-permute-start(f32[16]{0:T(128)S(1)} %get-tuple-element.336), channel_id=1, source_target_pairs={{0,64},{64,128},{128,192},{192,256},{256,320},{320,384},{384,448},... | collective-permute-start | bytes 200 | tf_op jit(solution)/shard_map/while/body/eval_jaxpr/ppermute | solution.py:10
  666.7 22.7 %collective-permute-start = (f32[16,16384]{1,0:T(8,128)}, f32[16,16384]{1,0:T(8,128)S(1)}, u32[]{:S(2)}, u32[]{:S(2)}) collective-permute-start(f32[16,16384]{1,0:T(8,128)} %fusion.23), channel_id=1, source_target_pairs={{0,64},{64,128},{128,192},{192,256},{256,320},{320,384},{384,448},... | collective-permute-start | bytes 3145736 | tf_op jit(solution)/shard_map/while/body/eval_jaxpr/ppermute | solution.py:10
  668.6 20.8 %collective-permute-start.1 = (f32[16]{0:T(128)S(1)}, f32[16]{0:T(128)S(1)}, u32[]{:S(2)}, u32[]{:S(2)}) collective-permute-start(f32[16]{0:T(128)S(1)} %get-tuple-element.336), channel_id=1, source_target_pairs={{0,64},{64,128},{128,192},{192,256},{256,320},{320,384},{384,448},... | collective-permute-start | bytes 200 | tf_op jit(solution)/shard_map/while/body/eval_jaxpr/ppermute | solution.py:10
  689.4 0.5 copy-start.2
  689.4 0.5 copy-start.3
